TPU v7x, 128 devices: a whole 4x4x4 slice. The times are simulated.
128 devices in a mesh: wide: 64 (over x, z, y), narrow: 2 (over core).
Axes of the slice: x: 4, y: 4, z: 4, core: 2. Of those that a mesh axis runs over, the one named last changes fastest.
Arguments:
- features: bfloat16 [16384, 512], P(('wide', 'narrow')), may hold values from -6 to 6
- weight: bfloat16 [512, 512], replicated, may hold values from -0.25 to 0.25
- tile_cols: int32 [128, 2, 48], P('wide', 'narrow'), may hold values from 0 to 63
- tile_count: int32 [128, 2], P('wide', 'narrow'), may hold values from 6 to 48, as said below
- tile_weights: bfloat16 [128, 2, 48, 128, 128], P('wide', 'narrow'), may hold values from 0 to 1, as said below
- cotangent: bfloat16 [16384, 512], P(('wide', 'narrow')), may hold values from -6 to 6
Outputs:
- activated: bfloat16 [16384, 512], P(('wide', 'narrow'))
- grad_features: bfloat16 [16384, 512], P(('wide', 'narrow'))
- grad_weight: float32 [512, 512], replicated
Inputs may be any that keep to these rules, and one draw needn't show every extreme that they name: `tile_count`: live slots of one tile row and residue; the largest equals 48 in every draw. `tile_weights`: edge weights; most entries of a tile are zero.
All inputs are finite; a program needn't handle non-finite values.
Results may differ from a plain program's by a relative error of at most 0.007.
Values may be sent and summed in bfloat16 or wider, within the bound.
No kernel may reach another device: no remote copies, remote signals or barrier semaphores. Data moves between devices by JAX's collectives and lax.ppermute only.
A program may use at most 128 MiB of HBM per device.

v0:
```python
import jax
import jax.numpy as jnp
from jax import lax
from jax.sharding import PartitionSpec as P


def per_device(features, weight, tile_cols, tile_count, tile_weights, cotangent):
    tile = features.shape[0]
    width = features.shape[1]
    copies = tile_cols.shape[0]
    slots = tile_cols.shape[2]
    owners = lax.axis_size("wide")
    columns = tile_cols[:, 0, :]
    counts = tile_count[:, 0]
    tiles = tile_weights[:, 0]
    gathered_features = lax.all_gather(features, "wide", axis=0, tiled=True)
    live = (jnp.arange(slots, dtype=jnp.int32)[None, :] < counts[:, None]).astype(jnp.bfloat16)
    onehot = (columns[..., None] == jnp.arange(owners, dtype=jnp.int32)).astype(
        jnp.bfloat16
    ) * live[..., None]
    dense = jnp.einsum("skj,sktc->stjc", onehot, tiles, preferred_element_type=jnp.float32).reshape(
        copies * tile, owners * tile
    )
    degree = 1.0 + lax.psum(jnp.sum(dense, axis=1), "narrow")
    scale = lax.rsqrt(degree)
    panel = dense.astype(jnp.bfloat16)
    panel_t = (
        jnp.einsum("skj,sktc->jcst", onehot, tiles, preferred_element_type=jnp.float32)
        .reshape(owners * tile, copies * tile)
        .astype(jnp.bfloat16)
    )
    cot_both = lax.all_gather(cotangent, "narrow", axis=0, tiled=True)
    panel, panel_t, scale, cot_both = lax.optimization_barrier((panel, panel_t, scale, cot_both))
    projected = jnp.dot(features, weight, preferred_element_type=jnp.float32).astype(jnp.bfloat16)
    own = lax.axis_index("narrow")
    aggregated = jnp.dot(panel, gathered_features, preferred_element_type=jnp.float32)
    partial_sum = jnp.dot(
        aggregated,
        weight.astype(jnp.float32),
        precision=lax.Precision.HIGHEST,
        preferred_element_type=jnp.float32,
    )
    selector = (jnp.arange(copies, dtype=jnp.int32) == own).astype(jnp.float32)
    self_term = selector[:, None, None] * projected.astype(jnp.float32)[None]
    partial_sum = partial_sum + self_term.reshape(copies * tile, width)
    pair = lax.axis_size("narrow")
    theirs = lax.ppermute(partial_sum, "narrow", [(i, pair - 1 - i) for i in range(pair)])
    preact_both = (partial_sum + theirs) * scale[:, None]
    sig = jax.nn.sigmoid(preact_both)
    cot_both = cot_both.astype(jnp.float32)
    all_grad = (cot_both * sig * (1.0 + preact_both * (1.0 - sig)) * scale[:, None]).astype(
        jnp.bfloat16
    )
    preact = lax.dynamic_slice_in_dim(preact_both, own * tile, tile, 0)
    activated = jax.nn.silu(preact).astype(jnp.bfloat16)
    own_grad = lax.dynamic_slice_in_dim(all_grad, own * tile, tile, 0)
    terms = jnp.dot(panel_t, all_grad, preferred_element_type=jnp.float32).astype(jnp.bfloat16)
    weight_terms = lax.dot_general(
        aggregated,
        all_grad.astype(jnp.float32),
        (((0,), (0,)), ((), ())),
        precision=lax.Precision.HIGHEST,
        preferred_element_type=jnp.float32,
    ) + lax.dot_general(
        features, own_grad, (((0,), (0,)), ((), ())), preferred_element_type=jnp.float32
    )
    rows = width // owners
    high = weight_terms.astype(jnp.bfloat16)
    low = (weight_terms - high.astype(jnp.float32)).astype(jnp.bfloat16)
    payload = jnp.concatenate(
        [
            terms.reshape(owners, tile, width),
            high.reshape(owners, rows, width),
            low.reshape(owners, rows, width),
        ],
        axis=1,
    )
    received = lax.all_to_all(payload, "wide", 0, 0, tiled=True)
    band = jnp.sum(
        received[:, tile : tile + rows].astype(jnp.float32)
        + received[:, tile + rows :].astype(jnp.float32),
        axis=0,
    )
    band = (band + lax.ppermute(band, "narrow", [(i, pair - 1 - i) for i in range(pair)])).astype(
        jnp.bfloat16
    )
    grad_weight = (
        lax.all_to_all(
            jnp.broadcast_to(band[None], (owners, rows, width)), "wide", 0, 0, tiled=True
        )
        .reshape(width, width)
        .astype(jnp.float32)
    )
    gathered_sum = jnp.sum(received[:, :tile].astype(jnp.float32), axis=0)
    message = (gathered_sum + own_grad.astype(jnp.float32)).astype(jnp.bfloat16)
    grad_features = lax.dot_general(
        message, weight, (((1,), (1,)), ((), ())), preferred_element_type=jnp.float32
    ).astype(jnp.bfloat16)
    return (activated, grad_features, grad_weight)


def solution(mesh):
    return jax.shard_map(
        per_device,
        mesh=mesh,
        in_specs=(
            P(("wide", "narrow"), None),
            P(),
            P("wide", "narrow", None),
            P("wide", "narrow"),
            P("wide", "narrow", None, None, None),
            P(("wide", "narrow"), None),
        ),
        out_specs=(P(("wide", "narrow"), None), P(("wide", "narrow"), None), P()),
        check_vma=False,
    )
```

profile of v0, /device:TPU:0, one launch (start us, length us, event | category | flops | bytes accessed | tf_op | source)
XLA Modules:
  0.0 263.9 jit_solution(4746101957128973760)
XLA Ops:
  7.2 0.7 all-gather.2.cloned.1.call-update
  7.9 0.9 compare_convert_fusion.1
  9.1 7.7 %fusion.16 = (bf16[2,64,128,128]{3,1,2,0:T(8,128)(2,1)}, bf16[2,128,64,128]{3,2,1,0:T(8,128)(2,1)}, f32[2,64,128,128]{3,1,2,0:T(8,128)S(1)}) fusion(bf16[2,48,128,128]{3,2,1,0:T(8,128)(2,1)S(1)} %bitcast.55, s32[2,48]{1,0:T(2,128)} %bitcast.60, bf16[2,48]{1,0:T(2,128)(2,1)S(1)} %compare_convert_fusion.1), kind=kOutput, calls=%fused_computation.41 | convolution fusion | flops 205533184 | bytes 19923520 | tf_op jit(solution)/shard_map/skj,sktc->stjc/dot_general | solution.py:21
  16.8 1.1 bitcast_reduce_fusion
  17.8 2.5 psum.7
  20.3 2.2 all_gather.6
  22.5 21.9 %copy_bitcast_fusion = (bf16[8192,256]{0,1:T(8,128)(2,1)}, bf16[256,8192]{1,0:T(8,128)(2,1)}) fusion(bf16[32,8,64,128]{3,2,1,0:T(8,128)(2,1)} %bitcast.57, bf16[32,8,64,128]{3,2,1,0:T(8,128)(2,1)} %bitcast.58), kind=kLoop, calls=%fused_computation.5 | loop fusion | bytes 16777216 | tf_op jit(solution)/shard_map/convert_element_type | solution.py:30
  44.8 47.0 %all-gather.2.cloned.1.call-done = bf16[8192,512]{1,0:T(8,128)(2,1)} async-done(((bf16[128,512]{1,0:T(8,128)(2,1)}), bf16[8192,512]{1,0:T(8,128)(2,1)}) %all-gather.2.cloned.1.call-update) | async-done | bytes 8388624 | tf_op jit(solution)/shard_map/all_gather | solution.py:16
  91.8 7.0 %fusion.19 = f32[256,512]{1,0:T(8,128)S(1)} fusion(bf16[256,8192]{1,0:T(8,128)(2,1)} %get-tuple-element.7, bf16[8192,512]{1,0:T(8,128)(2,1)} %all-gather.2.cloned.1.call-done), kind=kOutput, calls=%fused_computation.42 | convolution fusion | flops 2147483648 | bytes 13107200 | tf_op jit(solution)/shard_map/dot_general | solution.py:36
  98.8 0.6 convolution_add_fusion
  99.7 1.9 collective-permute-done
  101.9 0.6 fusion.20
  102.5 4.6 %convolution_convert_fusion = bf16[8192,512]{1,0:T(8,128)(2,1)S(1)} fusion(bf16[8192,256]{0,1:T(8,128)(2,1)} %get-tuple-element.9, bf16[256,512]{1,0:T(8,128)(2,1)S(1)} %get-tuple-element.11), kind=kOutput, calls=%fused_computation.1 | convolution fusion | flops 2151677952 | bytes 12845056 | tf_op jit(solution)/shard_map/dot_general | solution.py:57
  107.4 0.9 pad_maximum_fusion
  108.4 118.2 %all_to_all.10 = bf16[64,144,512]{2,1,0:T(8,128)(2,1)S(1)} all-to-all(bf16[64,144,512]{2,1,0:T(8,128)(2,1)S(1)} %pad_maximum_fusion), channel_id=1, replica_groups=mesh['wide'=64,'narrow'=2] {'wide'}, dimensions={0} | all-to-all | bytes 18874368 | tf_op jit(solution)/shard_map/all_to_all | solution.py:78
  226.6 3.6 %copy-done.2 = bf16[64,144,512]{2,1,0:T(8,128)(2,1)} copy-done((bf16[64,144,512]{2,1,0:T(8,128)(2,1)}, bf16[64,144,512]{2,1,0:T(8,128)(2,1)S(1)}, u32[]{:S(2)}) %copy-start.2) | copy-done | bytes 9437208
  230.5 0.7 multiply_convert_fusion.1
  231.2 0.4 collective-permute-done.1
  231.6 0.8 broadcast_in_dim.2
  232.5 9.1 %all-to-all-start.1 = ((bf16[64,8,512]{2,1,0:T(8,128)(2,1)}), bf16[64,8,512]{2,1,0:T(8,128)(2,1)}, u32[]{:S(2)}, u32[]{:S(2)}) async-start(bf16[64,8,512]{2,1,0:T(8,128)(2,1)} %broadcast_in_dim.2), calls=%async_computation.1 | async-start | bytes 1048576 | tf_op jit(solution)/shard_map/all_to_all | solution.py:88
  241.6 4.8 %convert_reduce_fusion = f32[128,512]{1,0:T(8,128)S(1)} fusion(bf16[64,144,512]{2,1,0:T(8,128)(2,1)} %copy-done.2), kind=kLoop, calls=%fused_computation | loop fusion | flops 8323072 | bytes 8650752 | tf_op jit(solution)/shard_map/reduce_sum | solution.py:94
  246.5 1.0 convolution_convert_fusion.1
  247.4 7.4 %all-to-all-done.1 = bf16[64,8,512]{2,1,0:T(8,128)(2,1)} async-done(((bf16[64,8,512]{2,1,0:T(8,128)(2,1)}), bf16[64,8,512]{2,1,0:T(8,128)(2,1)}, u32[]{:S(2)}, u32[]{:S(2)}) %all-to-all-start.1) | async-done | bytes 524320 | tf_op jit(solution)/shard_map/all_to_all | solution.py:88
  254.9 2.1 bitcast_convert_fusion.1
  (25 shorter events, 1.9 us)
Async XLA Ops:
  7.2 1.9 copy-start
  7.2 84.6 %all-gather.2.cloned.1.call-start = ((), (), s32[]{:S(2)}) async-start(), calls=%async_computation.2 | async-start | bytes 8519680 | tf_op jit(solution)/shard_map/all_gather | solution.py:16
  16.7 3.6 %copy-start.6 = (bf16[128,512]{1,0:T(8,128)(2,1)S(1)}, bf16[128,512]{1,0:T(8,128)(2,1)}, u32[]{:S(2)}) copy-start(bf16[128,512]{1,0:T(8,128)(2,1)} %param.11) | copy-start | bytes 393220
  22.5 22.0 %copy-start.3 = (bf16[512,512]{1,0:T(8,128)(2,1)S(1)}, bf16[512,512]{1,0:T(8,128)(2,1)}, u32[]{:S(2)}) copy-start(bf16[512,512]{1,0:T(8,128)(2,1)} %param.7) | copy-start | bytes 1572868
  22.5 22.0 %copy-start.5 = (bf16[128,512]{1,0:T(8,128)(2,1)S(1)}, bf16[128,512]{1,0:T(8,128)(2,1)}, u32[]{:S(2)}) copy-start(bf16[128,512]{1,0:T(8,128)(2,1)} %param.6) | copy-start | bytes 393220
  99.3 2.2 collective-permute-start
  108.4 148.7 %copy-start.1 = (bf16[2,1,48,128,128]{4,3,2,1,0:T(8,128)(2,1)S(1)}, bf16[2,1,48,128,128]{4,3,2,1,0:T(8,128)(2,1)}, u32[]{:S(2)}) copy-start(bf16[2,1,48,128,128]{4,3,2,1,0:T(8,128)(2,1)} %param.10) | copy-start | bytes 9437188
  226.6 3.6 %copy-start.2 = (bf16[64,144,512]{2,1,0:T(8,128)(2,1)}, bf16[64,144,512]{2,1,0:T(8,128)(2,1)S(1)}, u32[]{:S(2)}) copy-start(bf16[64,144,512]{2,1,0:T(8,128)(2,1)S(1)} %all_to_all.10) | copy-start | bytes 28311556
  230.4 1.3 collective-permute-start.1
  232.5 22.4 %all-to-all-start.1 = ((bf16[64,8,512]{2,1,0:T(8,128)(2,1)}), bf16[64,8,512]{2,1,0:T(8,128)(2,1)}, u32[]{:S(2)}, u32[]{:S(2)}) async-start(bf16[64,8,512]{2,1,0:T(8,128)(2,1)} %broadcast_in_dim.2), calls=%async_computation.1 | async-start | bytes 1048576 | tf_op jit(solution)/shard_map/all_to_all | solution.py:88
  241.6 4.9 %copy-start.4 = (bf16[512,512]{1,0:T(8,128)(2,1)S(1)}, bf16[512,512]{1,0:T(8,128)(2,1)}, u32[]{:S(2)}) copy-start(bf16[512,512]{1,0:T(8,128)(2,1)} %param.7) | copy-start | bytes 1572868
Sparse Core Ops, SparseCore 0:
  10.9 80.8 all-gather.1
where the time goes:
time: 264 us
  blocking collectives  123 us (47%)
  waiting for transfers between devices  57.4 us (22%)
  local copies, waits for them, and re-layouts  26.7 us (10%)
  matrix products  22 us (8%)
  between operations  14.2 us (5%)
  other arithmetic  11.2 us (4%)
  starting transfers between devices  9.54 us (4%)
    all_to_all x1, blocking collectives, per_device(): received = lax.all_to_all(payload, 'wide', 0, 0, tiled=True)  118 us
    all_gather x1, waiting for transfers between devices, per_device(): gathered_features = lax.all_gather(features, 'wide', axis=0, tiled=True)  47 us
    convert_element_type x1, local copies, waits for them, and re-layouts, per_device(): panel_t = jnp.einsum('skj,sktc->jcst', onehot, tiles, preferred_element_t...  21.9 us
    all_to_all x1, starting transfers between devices, per_device(): lax.all_to_all(jnp.broadcast_to(band[None], (owners, rows, width)), 'wide...  9.11 us
    dot_general x1, matrix products, per_device(): jnp.einsum('skj,sktc->stjc', onehot, tiles, preferred_element_type=jnp.fl...  7.69 us
    all_to_all x1, waiting for transfers between devices, per_device(): lax.all_to_all(jnp.broadcast_to(band[None], (owners, rows, width)), 'wide...  7.43 us
    dot_general x1, matrix products, per_device(): jnp.dot(panel, gathered_features, preferred_element_type=jnp.float32)  6.97 us
  transfers between devices with their start and end apart: 4, of which 4 were waited for; matrix products, arithmetic and copies ran while one was open for 15% of the time, Pallas kernels for 0%

commit v1 on v0

--- a/solution.py
+++ b/solution.py
@@ -13,7 +13,15 @@
     columns = tile_cols[:, 0, :]
     counts = tile_count[:, 0]
     tiles = tile_weights[:, 0]
-    gathered_features = lax.all_gather(features, "wide", axis=0, tiled=True)
+    gathered_features = jnp.concatenate(
+        lax.all_to_all(
+            jnp.stack(lax.axis_size("wide") * [features]),
+            axis_name="wide",
+            split_axis=0,
+            concat_axis=0,
+        ),
+        axis=0,
+    )
     live = (jnp.arange(slots, dtype=jnp.int32)[None, :] < counts[:, None]).astype(jnp.bfloat16)
     onehot = (columns[..., None] == jnp.arange(owners, dtype=jnp.int32)).astype(
         jnp.bfloat16

time: 264 us -> 311 us (1.18)
  waiting for transfers between devices: 57.4 us -> 85 us
  blocking collectives: 123 us -> 140 us
  between operations: 14.2 us -> 0.79 us
  starting transfers between devices: 9.54 us -> 21.4 us
  local copies, waits for them, and re-layouts: 26.7 us -> 31.6 us
    all_to_all x0 -> x1, waiting for transfers between devices: none -> 75.2 us  [per_device(): lax.all_to_all(jnp.stack(lax.axis_size('wide') * [features]), axis_name='...]
    all_gather x1 -> x0, waiting for transfers between devices: 47 us -> none  [per_device(): gathered_features = lax.all_gather(features, 'wide', axis=0, tiled=True)]
    all_to_all x1, blocking collectives: 118 us -> 135 us  [per_device(): received = lax.all_to_all(payload, 'wide', 0, 0, tiled=True)]
    all_to_all x0 -> x1, starting transfers between devices: none -> 11.9 us  [per_device(): lax.all_to_all(jnp.stack(lax.axis_size('wide') * [features]), axis_name='...]
    another operation x0 -> x1, local copies, waits for them, and re-layouts: none -> 5.29 us  [per_device(): jnp.stack(lax.axis_size('wide') * [features])]
  transfers between devices with their start and end apart: 4 -> 4, of which waited for: 4 -> 4; matrix products, arithmetic and copies ran while one was open for 15% -> 12% of each run, Pallas kernels for 0% -> 0%
where the time goes in v1:
time: 311 us
  blocking collectives  140 us (45%)
  waiting for transfers between devices  85 us (27%)
  local copies, waits for them, and re-layouts  31.6 us (10%)
  starting transfers between devices  21.4 us (7%)
  matrix products  21.3 us (7%)
  other arithmetic  10.4 us (3%)
    all_to_all x1, blocking collectives, per_device(): received = lax.all_to_all(payload, 'wide', 0, 0, tiled=True)  135 us
    all_to_all x1, waiting for transfers between devices, per_device(): lax.all_to_all(jnp.stack(lax.axis_size('wide') * [features]), axis_name='...  75.2 us
    convert_element_type x1, local copies, waits for them, and re-layouts, per_device(): panel_t = jnp.einsum('skj,sktc->jcst', onehot, tiles, preferred_element_t...  21.8 us
    all_to_all x1, starting transfers between devices, per_device(): lax.all_to_all(jnp.stack(lax.axis_size('wide') * [features]), axis_name='...  11.9 us
    all_to_all x1, starting transfers between devices, per_device(): lax.all_to_all(jnp.broadcast_to(band[None], (owners, rows, width)), 'wide...  9.11 us
    all_to_all x1, waiting for transfers between devices, per_device(): lax.all_to_all(jnp.broadcast_to(band[None], (owners, rows, width)), 'wide...  7.43 us
    dot_general x1, matrix products, per_device(): jnp.einsum('skj,sktc->stjc', onehot, tiles, preferred_element_type=jnp.fl...  6.98 us
    dot_general x1, matrix products, per_device(): jnp.dot(panel, gathered_features, preferred_element_type=jnp.float32)  6.97 us
  transfers between devices with their start and end apart: 4, of which 4 were waited for; matrix products, arithmetic and copies ran while one was open for 12% of the time, Pallas kernels for 0%

profile of v1, /device:TPU:0, one launch (start us, length us, event | category | flops | bytes accessed | tf_op | source)
XLA Modules:
  0.0 310.6 jit_solution(9089028174735625603)
XLA Ops:
  0.6 5.3 %stack.2 = bf16[64,128,512]{2,1,0:T(8,128)(2,1)} broadcast(bf16[128,512]{1,0:T(8,128)(2,1)} %param.6), dimensions={1,2} | broadcast | bytes 8519680 | tf_op jit(solution)/shard_map/stack | solution.py:18
  5.9 11.9 %all-to-all-start = ((bf16[64,128,512]{2,1,0:T(8,128)(2,1)}), bf16[64,128,512]{2,1,0:T(8,128)(2,1)}, u32[]{:S(2)}, u32[]{:S(2)}) async-start(bf16[64,128,512]{2,1,0:T(8,128)(2,1)} %stack.2), calls=%async_computation | async-start | bytes 16777216 | tf_op jit(solution)/shard_map/all_to_all | solution.py:17
  18.0 7.0 %fusion.16 = (bf16[2,64,128,128]{3,1,2,0:T(8,128)(2,1)}, bf16[2,128,64,128]{3,2,1,0:T(8,128)(2,1)}, f32[2,64,128,128]{3,1,2,0:T(8,128)S(1)}) fusion(bf16[2,48,128,128]{3,2,1,0:T(8,128)(2,1)S(1)} %bitcast.56, s32[2,48]{1,0:T(2,128)S(1)} %bitcast.61, bf16[2,48]{1,0:T(2,128)(2,1)S(1)} %compare_convert_fusion.1), kind=kOutput, calls=%fused_computation.41 | convolution fusion | flops 205533184 | bytes 19923520 | tf_op jit(solution)/shard_map/skj,sktc->stjc/dot_general | solution.py:29
  24.9 1.1 bitcast_reduce_fusion
  26.0 2.5 psum.7
  28.5 2.2 all_gather.3
  30.7 21.8 %copy_bitcast_fusion = (bf16[8192,256]{0,1:T(8,128)(2,1)}, bf16[256,8192]{1,0:T(8,128)(2,1)}) fusion(bf16[32,8,64,128]{3,2,1,0:T(8,128)(2,1)} %bitcast.58, bf16[32,8,64,128]{3,2,1,0:T(8,128)(2,1)} %bitcast.59), kind=kLoop, calls=%fused_computation.5 | loop fusion | bytes 16777216 | tf_op jit(solution)/shard_map/convert_element_type | solution.py:38
  52.9 75.2 %all-to-all-done = bf16[64,128,512]{2,1,0:T(8,128)(2,1)} async-done(((bf16[64,128,512]{2,1,0:T(8,128)(2,1)}), bf16[64,128,512]{2,1,0:T(8,128)(2,1)}, u32[]{:S(2)}, u32[]{:S(2)}) %all-to-all-start) | async-done | bytes 8388640 | tf_op jit(solution)/shard_map/all_to_all | solution.py:17
  128.1 7.0 %fusion.19 = f32[256,512]{1,0:T(8,128)S(1)} fusion(bf16[256,8192]{1,0:T(8,128)(2,1)} %get-tuple-element.7, bf16[8192,512]{1,0:T(8,128)(2,1)} %bitcast.8), kind=kOutput, calls=%fused_computation.42 | convolution fusion | flops 2147483648 | bytes 13107200 | tf_op jit(solution)/shard_map/dot_general | solution.py:44
  135.1 0.6 convolution_add_fusion
  136.0 1.9 collective-permute-done
  138.2 0.6 fusion.20
  138.8 4.6 %convolution_convert_fusion = bf16[8192,512]{1,0:T(8,128)(2,1)S(1)} fusion(bf16[8192,256]{0,1:T(8,128)(2,1)} %get-tuple-element.9, bf16[256,512]{1,0:T(8,128)(2,1)S(1)} %get-tuple-element.11), kind=kOutput, calls=%fused_computation.1 | convolution fusion | flops 2151677952 | bytes 12845056 | tf_op jit(solution)/shard_map/dot_general | solution.py:65
  143.8 0.9 pad_maximum_fusion
  144.7 135.5 %all_to_all.15 = bf16[64,144,512]{2,1,0:T(8,128)(2,1)S(1)} all-to-all(bf16[64,144,512]{2,1,0:T(8,128)(2,1)S(1)} %pad_maximum_fusion), channel_id=1, replica_groups=mesh['wide'=64,'narrow'=2] {'wide'}, dimensions={0} | all-to-all | bytes 18874368 | tf_op jit(solution)/shard_map/all_to_all | solution.py:86
  280.2 3.6 %copy-done.2 = bf16[64,144,512]{2,1,0:T(8,128)(2,1)} copy-done((bf16[64,144,512]{2,1,0:T(8,128)(2,1)}, bf16[64,144,512]{2,1,0:T(8,128)(2,1)S(1)}, u32[]{:S(2)}) %copy-start.2) | copy-done | bytes 9437208
  284.0 0.7 multiply_convert_fusion.1
  284.8 0.4 collective-permute-done.1
  285.2 0.8 broadcast_in_dim.2
  286.0 9.1 %all-to-all-start.2 = ((bf16[64,8,512]{2,1,0:T(8,128)(2,1)}), bf16[64,8,512]{2,1,0:T(8,128)(2,1)}, u32[]{:S(2)}, u32[]{:S(2)}) async-start(bf16[64,8,512]{2,1,0:T(8,128)(2,1)} %broadcast_in_dim.2), calls=%async_computation.2 | async-start | bytes 1048576 | tf_op jit(solution)/shard_map/all_to_all | solution.py:96
  295.2 4.8 %convert_reduce_fusion = f32[128,512]{1,0:T(8,128)S(1)} fusion(bf16[64,144,512]{2,1,0:T(8,128)(2,1)} %copy-done.2), kind=kLoop, calls=%fused_computation | loop fusion | flops 8323072 | bytes 8650752 | tf_op jit(solution)/shard_map/reduce_sum | solution.py:102
  300.0 1.0 convolution_convert_fusion.1
  301.0 7.4 %all-to-all-done.2 = bf16[64,8,512]{2,1,0:T(8,128)(2,1)} async-done(((bf16[64,8,512]{2,1,0:T(8,128)(2,1)}), bf16[64,8,512]{2,1,0:T(8,128)(2,1)}, u32[]{:S(2)}, u32[]{:S(2)}) %all-to-all-start.2) | async-done | bytes 524320 | tf_op jit(solution)/shard_map/all_to_all | solution.py:96
  308.4 2.1 bitcast_convert_fusion.1
  (29 shorter events, 1.7 us)
Async XLA Ops:
  0.6 17.3 %copy-start = (bf16[2,1,48,128,128]{4,3,2,1,0:T(8,128)(2,1)S(1)}, bf16[2,1,48,128,128]{4,3,2,1,0:T(8,128)(2,1)}, u32[]{:S(2)}) copy-start(bf16[2,1,48,128,128]{4,3,2,1,0:T(8,128)(2,1)} %param.10) | copy-start | bytes 9437188
  5.9 11.9 %copy-start.8 = (s32[2,1]{0,1:T(1,128)S(1)}, s32[2,1]{0,1:T(1,128)}, u32[]{:S(2)}) copy-start(s32[2,1]{0,1:T(1,128)} %param.9) | copy-start | bytes 28
  5.9 12.0 %copy-start.7 = (s32[2,1,48]{2,1,0:T(1,128)S(1)}, s32[2,1,48]{2,1,0:T(1,128)}, u32[]{:S(2)}) copy-start(s32[2,1,48]{2,1,0:T(1,128)} %param.8) | copy-start | bytes 1156
  5.9 122.2 %all-to-all-start = ((bf16[64,128,512]{2,1,0:T(8,128)(2,1)}), bf16[64,128,512]{2,1,0:T(8,128)(2,1)}, u32[]{:S(2)}, u32[]{:S(2)}) async-start(bf16[64,128,512]{2,1,0:T(8,128)(2,1)} %stack.2), calls=%async_computation | async-start | bytes 16777216 | tf_op jit(solution)/shard_map/all_to_all | solution.py:17
  24.9 3.6 %copy-start.6 = (bf16[128,512]{1,0:T(8,128)(2,1)S(1)}, bf16[128,512]{1,0:T(8,128)(2,1)}, u32[]{:S(2)}) copy-start(bf16[128,512]{1,0:T(8,128)(2,1)} %param.11) | copy-start | bytes 393220
  30.7 21.9 %copy-start.3 = (bf16[512,512]{1,0:T(8,128)(2,1)S(1)}, bf16[512,512]{1,0:T(8,128)(2,1)}, u32[]{:S(2)}) copy-start(bf16[512,512]{1,0:T(8,128)(2,1)} %param.7) | copy-start | bytes 1572868
  30.7 21.9 %copy-start.5 = (bf16[128,512]{1,0:T(8,128)(2,1)S(1)}, bf16[128,512]{1,0:T(8,128)(2,1)}, u32[]{:S(2)}) copy-start(bf16[128,512]{1,0:T(8,128)(2,1)} %param.6) | copy-start | bytes 393220
  135.7 2.2 collective-permute-start
  144.7 165.9 %copy-start.1 = (bf16[2,1,48,128,128]{4,3,2,1,0:T(8,128)(2,1)S(1)}, bf16[2,1,48,128,128]{4,3,2,1,0:T(8,128)(2,1)}, u32[]{:S(2)}) copy-start(bf16[2,1,48,128,128]{4,3,2,1,0:T(8,128)(2,1)} %param.10) | copy-start | bytes 9437188
  280.2 3.6 %copy-start.2 = (bf16[64,144,512]{2,1,0:T(8,128)(2,1)}, bf16[64,144,512]{2,1,0:T(8,128)(2,1)S(1)}, u32[]{:S(2)}) copy-start(bf16[64,144,512]{2,1,0:T(8,128)(2,1)S(1)} %all_to_all.15) | copy-start | bytes 28311556
  283.9 1.3 collective-permute-start.1
  286.0 22.4 %all-to-all-start.2 = ((bf16[64,8,512]{2,1,0:T(8,128)(2,1)}), bf16[64,8,512]{2,1,0:T(8,128)(2,1)}, u32[]{:S(2)}, u32[]{:S(2)}) async-start(bf16[64,8,512]{2,1,0:T(8,128)(2,1)} %broadcast_in_dim.2), calls=%async_computation.2 | async-start | bytes 1048576 | tf_op jit(solution)/shard_map/all_to_all | solution.py:96
  295.2 4.9 %copy-start.4 = (bf16[512,512]{1,0:T(8,128)(2,1)S(1)}, bf16[512,512]{1,0:T(8,128)(2,1)}, u32[]{:S(2)}) copy-start(bf16[512,512]{1,0:T(8,128)(2,1)} %param.7) | copy-start | bytes 1572868
